TPU v7x, 256 devices: a whole 4x4x8 slice. The times are simulated.
256 devices in a mesh: pos: 16 (over x_hi, z), exp: 16 (over y, x_lo, core).
Axes of the slice: x: 4 (x_hi: 2, x_lo: 2; x = x_hi * 2 + x_lo), y: 4, z: 8, core: 2. Of those that a mesh axis runs over, the one named last changes fastest.
Arguments:
- patches: bfloat16 [65536, 4, 256], P(('pos', 'exp')), may hold values from -6 to 6
- conv_weight: bfloat16 [3, 256, 2048], replicated, may hold values from -0.21875 to 0.21875
- phi: bfloat16 [2048, 128], replicated, may hold values from -40 to 40, as said below
- w_in: bfloat16 [16, 2048, 8192], P('exp', None, 'pos'), may hold values from -0.125 to 0.125
- w_out: bfloat16 [16, 8192, 2048], P('exp', 'pos'), may hold values from -0.0625 to 0.0625
Outputs:
- mixed: bfloat16 [65536, 4, 2048], P(('pos', 'exp'))
Inputs may be any that keep to these rules, and one draw needn't show every extreme that they name: phi is real-valued.
All inputs are finite; a program needn't handle non-finite values.
Results may differ from a plain program's by a relative error of at most 0.019.
The roundings to bfloat16 on the way count: a program that leaves them out, or rounds other values in their place, can miss the bound.
Values may be sent and summed in bfloat16 or wider, within the bound.
No kernel may reach another device: no remote copies, remote signals or barrier semaphores. Data moves between devices by JAX's collectives and lax.ppermute only.
A program may use at most 128 MiB of HBM per device.

v0:
```python
import jax
import jax.numpy as jnp
from jax import lax
from jax.sharding import PartitionSpec as P

D = 2048
SLOTS_PER = 8


def with_halo(array, sides, width):
    for axis, dim in sides:
        count, length = (lax.axis_size(axis), array.shape[dim])
        up = [(i, (i + 1) % count) for i in range(count - 1)]
        down = [(j, i) for i, j in up]
        last = lax.slice_in_dim(array, length - width, length, axis=dim)
        initial = lax.slice_in_dim(array, 0, width, axis=dim)
        before = lax.ppermute(last, axis, up)
        after = lax.ppermute(initial, axis, down)
        array = jnp.concatenate([before, array, after], axis=dim)
    return array


def per_device(patches, conv_weight, phi, w_in, w_out):
    channels, periods, samples = patches.shape
    padded = with_halo(patches, ((("pos", "exp"), 0),), 1)
    running = jnp.zeros((channels * periods, D), jnp.float32)
    for offset in range(3):
        window = padded[offset : offset + channels].reshape(channels * periods, samples)
        running = running + jnp.dot(window, conv_weight[offset], preferred_element_type=jnp.float32)
    flat = running.astype(jnp.bfloat16)
    logits = jnp.dot(flat, phi, preferred_element_type=jnp.float32)
    local_peak = jnp.max(logits, axis=0)
    column_peak = lax.pmax(local_peak, ("pos", "exp"))
    raw_weights = jnp.exp(logits - column_peak)
    column_total = lax.psum(jnp.sum(raw_weights, axis=0), ("pos", "exp"))
    dispatch = (raw_weights / column_total).astype(jnp.bfloat16)
    group = lax.axis_index("exp")
    every_slot = lax.dot_general(
        dispatch, flat, (((0,), (0,)), ((), ())), preferred_element_type=jnp.float32
    )
    summed = lax.psum(every_slot, ("pos", "exp"))
    owned = lax.dynamic_slice_in_dim(summed, group * SLOTS_PER, SLOTS_PER, 0)
    slot_in = owned.astype(jnp.bfloat16)
    hidden = jax.nn.gelu(
        jnp.dot(slot_in, w_in[0], preferred_element_type=jnp.float32), approximate=True
    ).astype(jnp.bfloat16)
    expert_term = jnp.dot(hidden, w_out[0], preferred_element_type=jnp.float32)
    slot_out = lax.psum(expert_term, "pos").astype(jnp.bfloat16)
    row_peak = jnp.max(logits, axis=1, keepdims=True)
    row_weights = jnp.exp(logits - row_peak)
    combine = (row_weights / jnp.sum(row_weights, axis=1, keepdims=True)).astype(jnp.bfloat16)
    mixed = jnp.dot(
        combine,
        lax.all_gather(slot_out, "exp", axis=0, tiled=True),
        preferred_element_type=jnp.float32,
    )
    return mixed.astype(jnp.bfloat16).reshape(channels, periods, D)


def solution(mesh):
    in_specs = (
        P(("pos", "exp"), None, None),
        P(),
        P(),
        P("exp", None, "pos"),
        P("exp", "pos", None),
    )
    out_specs = P(("pos", "exp"), None, None)
    return jax.shard_map(
        per_device, mesh=mesh, in_specs=in_specs, out_specs=out_specs, check_vma=False
    )
```

profile of v0, /device:TPU:1, one launch (start us, length us, event | category | flops | bytes accessed | tf_op | source)
XLA Modules:
  0.0 376.0 jit_solution(2195007920341952127)
XLA Ops:
  0.0 0.9 fusion.47
  0.9 4.5 %collective-permute-start = (bf16[1,4,256]{2,1,0:T(4,128)(2,1)S(1)}, bf16[1,4,256]{2,1,0:T(4,128)(2,1)S(1)}, u32[]{:S(2)}, u32[]{:S(2)}) collective-permute-start(bf16[1,4,256]{2,1,0:T(4,128)(2,1)S(1)} %get-tuple-element.12), channel_id=1, source_target_pairs={{0,1},{1,2},{2,3},{3,4},{4,5},{5,6},{6,7},{7,8},{8,9},{9,10},{10,1... | collective-permute-start | bytes 6152 | tf_op jit(solution)/shard_map/ppermute | solution.py:17
  5.3 1.9 collective-permute-start.1
  7.3 1.2 reshape.17
  8.5 5.8 %fusion.8 = f32[1024,2048]{1,0:T(8,128)} fusion(bf16[1024,256]{1,0:T(8,128)(2,1)S(1)} %reshape.17, bf16[3,256,2048]{2,1,0:T(8,128)(2,1)} %param.6), kind=kOutput, calls=%fused_computation.8 | convolution fusion | flops 1073741824 | bytes 9961472 | tf_op jit(solution)/shard_map/dot_general | solution.py:29
  14.2 1.3 pad_maximum_fusion
  15.6 1.2 reshape.16
  16.7 0.0 copy-start.3
  16.8 5.8 %fusion.10 = f32[1024,2048]{1,0:T(8,128)} fusion(bf16[1024,256]{1,0:T(8,128)(2,1)S(1)} %reshape.16, bf16[3,256,2048]{2,1,0:T(8,128)(2,1)} %param.6), kind=kOutput, calls=%fused_computation.10 | convolution fusion | flops 1073741824 | bytes 9961472 | tf_op jit(solution)/shard_map/dot_general | solution.py:29
  22.5 0.1 reshape.18
  22.7 7.4 %add_convert_fusion = bf16[1024,2048]{1,0:T(8,128)(2,1)S(1)} fusion(f32[1024,2048]{1,0:T(8,128)} %fusion.10, f32[1024,2048]{1,0:T(8,128)} %fusion.8, bf16[1024,256]{1,0:T(8,128)(2,1)S(1)} %reshape.18, bf16[3,256,2048]{2,1,0:T(8,128)(2,1)} %param.6), kind=kOutput, calls=%fused_computation | convolution fusion | flops 1080033280 | bytes 22544384 | tf_op jit(solution)/shard_map/dot_general | solution.py:29
  30.0 0.0 copy-start.1
  30.1 2.0 copy-done.1
  32.1 1.3 fusion.46
  33.4 80.7 %pmax.7 = f32[128]{0:T(128)S(1)} all-reduce(f32[128]{0:T(128)S(1)} %get-tuple-element.8), channel_id=1, replica_groups=mesh['pos'=16,'exp'=16] {'pos','exp'}, use_global_device_ids=true, to_apply=%region_3.0 | all-reduce | flops 128 | bytes 1024 | tf_op jit(solution)/shard_map/pmax | solution.py:33
  114.1 0.4 fusion.15
  114.5 72.9 %psum.21 = f32[128]{0:T(128)S(1)} all-reduce(f32[128]{0:T(128)S(1)} %get-tuple-element.6), channel_id=1, replica_groups=mesh['pos'=16,'exp'=16] {'pos','exp'}, use_global_device_ids=true, to_apply=%region_5.0 | all-reduce | flops 128 | bytes 1024 | tf_op jit(solution)/shard_map/psum | solution.py:35
  187.4 3.9 %fusion.17 = f32[128,2048]{1,0:T(8,128)} fusion(bf16[1024,2048]{1,0:T(8,128)(2,1)} %copy-done.1, f32[1024,128]{1,0:T(8,128)S(1)} %get-tuple-element.13, f32[128]{0:T(128)S(1)} %psum.21, f32[128]{0:T(128)S(1)} %pmax.7), kind=kOutput, calls=%fused_computation.23 | convolution fusion | flops 537264128 | bytes 5768192 | tf_op jit(solution)/shard_map/dot_general | solution.py:38
  191.3 78.0 %all-reduce.1 = bf16[128,2048]{1,0:T(8,128)(2,1)S(1)} all-reduce(f32[128,2048]{1,0:T(8,128)} %fusion.17), channel_id=1, replica_groups=mesh['pos'=16,'exp'=16] {'pos','exp'}, use_global_device_ids=true, to_apply=%region_6.0 | all-reduce | flops 262144 | bytes 1572864 | tf_op jit(solution)/shard_map/psum | solution.py:41
  269.4 2.3 fusion
  271.7 62.1 %psum.23 = bf16[8,2048]{1,0:T(8,128)(2,1)S(1)} all-reduce(f32[8,2048]{1,0:T(8,128)S(1)} %fusion), channel_id=1, replica_groups=mesh['pos'=16,'exp'=16] {'pos'}, use_global_device_ids=true, to_apply=%region_7.0 | all-reduce | flops 16384 | bytes 98304 | tf_op jit(solution)/shard_map/psum | solution.py:48
  333.8 31.7 %all_gather.3 = bf16[128,2048]{1,0:T(8,128)(2,1)S(1)} all-gather(bf16[8,2048]{1,0:T(8,128)(2,1)S(1)} %psum.23), channel_id=1, replica_groups=mesh['pos'=16,'exp'=16] {'exp'}, dimensions={0}, use_global_device_ids=true | all-gather | bytes 557056 | tf_op jit(solution)/shard_map/all_gather | solution.py:54
  365.6 3.3 convolution_convert_fusion
  368.8 7.2 %reshape.19 = bf16[256,4,2048]{2,1,0:T(4,128)(2,1)} reshape(bf16[1024,2048]{1,0:T(8,128)(2,1)} %convolution_convert_fusion) | data formatting | bytes 8388608 | tf_op jit(solution)/shard_map/reshape | solution.py:57
  (9 shorter events, 0.0 us)
Async XLA Ops:
  0.0 269.4 %copy-start = (bf16[1,512,2048]{2,1,0:T(8,128)(2,1)S(1)}, bf16[1,512,2048]{2,1,0:T(8,128)(2,1)}, u32[]{:S(2)}) copy-start(bf16[1,512,2048]{2,1,0:T(8,128)(2,1)} %param.9) | copy-start | bytes 6291460
  0.9 13.4 %collective-permute-start = (bf16[1,4,256]{2,1,0:T(4,128)(2,1)S(1)}, bf16[1,4,256]{2,1,0:T(4,128)(2,1)S(1)}, u32[]{:S(2)}, u32[]{:S(2)}) collective-permute-start(bf16[1,4,256]{2,1,0:T(4,128)(2,1)S(1)} %get-tuple-element.12), channel_id=1, source_target_pairs={{0,1},{1,2},{2,3},{3,4},{4,5},{5,6},{6,7},{7,8},{8,9},{9,10},{10,1... | collective-permute-start | bytes 6152 | tf_op jit(solution)/shard_map/ppermute | solution.py:17
  5.3 8.9 %collective-permute-start.1 = (bf16[1,4,256]{2,1,0:T(4,128)(2,1)S(1)}, bf16[1,4,256]{2,1,0:T(4,128)(2,1)S(1)}, u32[]{:S(2)}, u32[]{:S(2)}) collective-permute-start(bf16[1,4,256]{2,1,0:T(4,128)(2,1)S(1)} %get-tuple-element.11), channel_id=1, source_target_pairs={{1,0},{2,1},{3,2},{4,3},{5,4},{6,5},{7,6},{8,7},{9,8},{10,9},{11,1... | collective-permute-start | bytes 6152 | tf_op jit(solution)/shard_map/ppermute | solution.py:18
  8.4 5.8 %copy-start.2 = (bf16[256,4,256]{2,1,0:T(4,128)(2,1)S(1)}, bf16[256,4,256]{2,1,0:T(4,128)(2,1)}, u32[]{:S(2)}) copy-start(bf16[256,4,256]{2,1,0:T(4,128)(2,1)} %param.5) | copy-start | bytes 1572868
  16.7 5.8 %copy-start.3 = (bf16[256,4,256]{2,1,0:T(4,128)(2,1)S(1)}, bf16[256,4,256]{2,1,0:T(4,128)(2,1)}, u32[]{:S(2)}) copy-start(bf16[256,4,256]{2,1,0:T(4,128)(2,1)} %get-tuple-element.9) | copy-start | bytes 1572868
  22.6 9.4 %copy-start.4 = (bf16[2048,128]{1,0:T(8,128)(2,1)S(1)}, bf16[2048,128]{1,0:T(8,128)(2,1)}, u32[]{:S(2)}) copy-start(bf16[2048,128]{1,0:T(8,128)(2,1)} %param.7) | copy-start | bytes 1572868
  30.0 2.0 copy-start.1
where the time goes:
time: 377 us; the launch traced here: 376 us
  blocking collectives  326 us (86%)
  matrix products  29.8 us (8%)
  local copies, waits for them, and re-layouts  12.5 us (3%)
  starting transfers between devices  6.41 us (2%)
    pmax x1, blocking collectives, per_device(): column_peak = lax.pmax(local_peak, ('pos', 'exp'))  80.7 us
    psum x1, blocking collectives, per_device(): summed = lax.psum(every_slot, ('pos', 'exp'))  78 us
    psum x1, blocking collectives, per_device(): column_total = lax.psum(jnp.sum(raw_weights, axis=0), ('pos', 'exp'))  72.9 us
    psum x1, blocking collectives, per_device(): slot_out = lax.psum(expert_term, 'pos').astype(jnp.bfloat16)  62.1 us
    all_gather x1, blocking collectives, per_device(): lax.all_gather(slot_out, 'exp', axis=0, tiled=True)  31.7 us
    dot_general x3, matrix products, per_device(): jnp.dot(window, conv_weight[offset], preferred_element_type=jnp.float32)  18.9 us
  transfers between devices with their start and end apart: 2, of which 0 were waited for; matrix products, arithmetic and copies ran while one was open for 2% of the time, Pallas kernels for 0%

commit v1 on v0

--- a/solution.py
+++ b/solution.py
@@ -5,6 +5,7 @@
 
 D = 2048
 SLOTS_PER = 8
+fit_run_all = lambda vec, bus_axis: jnp.sum(lax.all_gather(vec, bus_axis), axis=0)
 
 
 def with_halo(array, sides, width):
@@ -32,7 +33,7 @@
     local_peak = jnp.max(logits, axis=0)
     column_peak = lax.pmax(local_peak, ("pos", "exp"))
     raw_weights = jnp.exp(logits - column_peak)
-    column_total = lax.psum(jnp.sum(raw_weights, axis=0), ("pos", "exp"))
+    column_total = fit_run_all(jnp.sum(raw_weights, axis=0), ("pos", "exp"))
     dispatch = (raw_weights / column_total).astype(jnp.bfloat16)
     group = lax.axis_index("exp")
     every_slot = lax.dot_general(

time: 377 us -> 643 us (1.71)
  blocking collectives: 326 us -> 592 us
    all_gather x0 -> x1, blocking collectives: none -> 341 us  [lax.all_gather(vec, bus_axis)]
    psum x1 -> x0, blocking collectives: 72.9 us -> none  [per_device(): column_total = lax.psum(jnp.sum(raw_weights, axis=0), ('pos', 'exp'))]
  transfers between devices with their start and end apart: 2 -> 2, of which waited for: 0 -> 0; matrix products, arithmetic and copies ran while one was open for 2% -> 1% of each run, Pallas kernels for 0% -> 0%
where the time goes in v1:
time: 643 us
  blocking collectives  592 us (92%)
  matrix products  29.7 us (5%)
  local copies, waits for them, and re-layouts  12.5 us (2%)
    all_gather x1, blocking collectives, lax.all_gather(vec, bus_axis)  341 us
    pmax x1, blocking collectives, per_device(): column_peak = lax.pmax(local_peak, ('pos', 'exp'))  80.7 us
    psum x1, blocking collectives, per_device(): summed = lax.psum(every_slot, ('pos', 'exp'))  75.9 us
    psum x1, blocking collectives, per_device(): slot_out = lax.psum(expert_term, 'pos').astype(jnp.bfloat16)  61.8 us
    all_gather x1, blocking collectives, per_device(): lax.all_gather(slot_out, 'exp', axis=0, tiled=True)  32.4 us
    dot_general x3, matrix products, per_device(): jnp.dot(window, conv_weight[offset], preferred_element_type=jnp.float32)  18.9 us
  transfers between devices with their start and end apart: 2, of which 0 were waited for; matrix products, arithmetic and copies ran while one was open for 1% of the time, Pallas kernels for 0%

profile of v1, /device:TPU:1, one launch (start us, length us, event | category | flops | bytes accessed | tf_op | source)
XLA Modules:
  0.0 642.8 jit_solution(12792812096105564002)
XLA Ops:
  0.0 0.9 fusion.47
  0.9 4.5 collective-permute-start
  5.3 1.9 collective-permute-start.1
  7.3 1.2 reshape.17
  8.5 5.8 fusion.8
  14.2 1.3 pad_maximum_fusion
  15.6 1.2 reshape.16
  16.7 0.0 copy-start.3
  16.8 5.8 fusion.10
  22.5 0.1 reshape.18
  22.7 7.4 %add_convert_fusion = bf16[1024,2048]{1,0:T(8,128)(2,1)S(1)} fusion(f32[1024,2048]{1,0:T(8,128)} %fusion.10, f32[1024,2048]{1,0:T(8,128)} %fusion.8, bf16[1024,256]{1,0:T(8,128)(2,1)S(1)} %reshape.18, bf16[3,256,2048]{2,1,0:T(8,128)(2,1)} %param.6), kind=kOutput, calls=%fused_computation | convolution fusion | flops 1080033280 | bytes 22544384 | tf_op jit(solution)/shard_map/dot_general | solution.py:30
  30.1 2.0 copy-done.1
  32.1 1.3 fusion.46
  33.4 80.7 %pmax.7 = f32[128]{0:T(128)S(1)} all-reduce(f32[128]{0:T(128)S(1)} %get-tuple-element.8), channel_id=1, replica_groups=mesh['pos'=16,'exp'=16] {'pos','exp'}, use_global_device_ids=true, to_apply=%region_3.0 | all-reduce | flops 128 | bytes 1024 | tf_op jit(solution)/shard_map/pmax | solution.py:34
  114.1 0.4 fusion.15
  114.5 341.2 %all-gather.1 = f32[256,1,128]{2,1,0:T(1,128)S(1)} all-gather(f32[1,1,128]{2,1,0:T(1,128)S(1)} %bitcast.31), channel_id=2, replica_groups=mesh['pos'=16,'exp'=16] {'pos','exp'}, dimensions={0}, use_global_device_ids=true | all-gather | bytes 131584 | tf_op jit(solution)/shard_map/all_gather | solution.py:8
  455.7 0.3 reduce_sum.29
  455.9 3.9 fusion.17
  459.9 75.9 %all-reduce.1 = bf16[128,2048]{1,0:T(8,128)(2,1)S(1)} all-reduce(f32[128,2048]{1,0:T(8,128)} %fusion.17), channel_id=1, replica_groups=mesh['pos'=16,'exp'=16] {'pos','exp'}, use_global_device_ids=true, to_apply=%region_6.0 | all-reduce | flops 262144 | bytes 1572864 | tf_op jit(solution)/shard_map/psum | solution.py:42
  535.8 2.3 fusion
  538.1 61.8 %psum.15 = bf16[8,2048]{1,0:T(8,128)(2,1)S(1)} all-reduce(f32[8,2048]{1,0:T(8,128)S(1)} %fusion), channel_id=1, replica_groups=mesh['pos'=16,'exp'=16] {'pos'}, use_global_device_ids=true, to_apply=%region_7.0 | all-reduce | flops 16384 | bytes 98304 | tf_op jit(solution)/shard_map/psum | solution.py:49
  600.0 32.4 %all_gather.11 = bf16[128,2048]{1,0:T(8,128)(2,1)S(1)} all-gather(bf16[8,2048]{1,0:T(8,128)(2,1)S(1)} %psum.15), channel_id=1, replica_groups=mesh['pos'=16,'exp'=16] {'exp'}, dimensions={0}, use_global_device_ids=true | all-gather | bytes 557056 | tf_op jit(solution)/shard_map/all_gather | solution.py:55
  632.3 3.2 convolution_convert_fusion
  635.6 7.2 %reshape.19 = bf16[256,4,2048]{2,1,0:T(4,128)(2,1)} reshape(bf16[1024,2048]{1,0:T(8,128)(2,1)} %convolution_convert_fusion) | data formatting | bytes 8388608 | tf_op jit(solution)/shard_map/reshape | solution.py:58
  (10 shorter events, 0.0 us)
Async XLA Ops:
  0.0 535.8 %copy-start = (bf16[1,512,2048]{2,1,0:T(8,128)(2,1)S(1)}, bf16[1,512,2048]{2,1,0:T(8,128)(2,1)}, u32[]{:S(2)}) copy-start(bf16[1,512,2048]{2,1,0:T(8,128)(2,1)} %param.9) | copy-start | bytes 6291460
  0.9 13.4 %collective-permute-start = (bf16[1,4,256]{2,1,0:T(4,128)(2,1)S(1)}, bf16[1,4,256]{2,1,0:T(4,128)(2,1)S(1)}, u32[]{:S(2)}, u32[]{:S(2)}) collective-permute-start(bf16[1,4,256]{2,1,0:T(4,128)(2,1)S(1)} %get-tuple-element.12), channel_id=1, source_target_pairs={{0,1},{1,2},{2,3},{3,4},{4,5},{5,6},{6,7},{7,8},{8,9},{9,10},{10,1... | collective-permute-start | bytes 6152 | tf_op jit(solution)/shard_map/ppermute | solution.py:18
  5.3 8.9 %collective-permute-start.1 = (bf16[1,4,256]{2,1,0:T(4,128)(2,1)S(1)}, bf16[1,4,256]{2,1,0:T(4,128)(2,1)S(1)}, u32[]{:S(2)}, u32[]{:S(2)}) collective-permute-start(bf16[1,4,256]{2,1,0:T(4,128)(2,1)S(1)} %get-tuple-element.11), channel_id=1, source_target_pairs={{1,0},{2,1},{3,2},{4,3},{5,4},{6,5},{7,6},{8,7},{9,8},{10,9},{11,1... | collective-permute-start | bytes 6152 | tf_op jit(solution)/shard_map/ppermute | solution.py:19
  8.4 5.8 copy-start.2
  16.7 5.8 copy-start.3
  22.6 9.4 %copy-start.4 = (bf16[2048,128]{1,0:T(8,128)(2,1)S(1)}, bf16[2048,128]{1,0:T(8,128)(2,1)}, u32[]{:S(2)}) copy-start(bf16[2048,128]{1,0:T(8,128)(2,1)} %param.7) | copy-start | bytes 1572868
  30.0 2.0 copy-start.1
